TPU v7x, 512 devices: a whole 4x8x8 slice. The times are simulated.
512 devices in a mesh: dom: 128 (over z, y, core), feat: 4 (over x).
Axes of the slice: x: 4, y: 8, z: 8, core: 2. Of those that a mesh axis runs over, the one named last changes fastest.
Arguments:
- node_feats: bfloat16 [256, 262144], P('feat', 'dom'), may hold values from -6 to 6
- weight: bfloat16 [256, 256], P(None, 'feat'), may hold values from -0.375 to 0.375
- bias_vec: bfloat16 [256], P('feat'), may hold values from -3 to 3
- adj_tiles: bfloat16 [12288, 128, 128], P('dom'), may hold values from -0.25 to 0.25
- tile_row: int32 [12288], P('dom'), may hold values from 0 to 15, as said below
- tile_col: int32 [12288], P('dom'), may hold values from 0 to 143, as said below
- tile_count: int32 [128], P('dom'), may hold values from 58 to 96
- send_block: int32 [16384], P('dom'), may hold values from 0 to 15, as said below
- cotangent: bfloat16 [256, 262144], P('feat', 'dom'), may hold values from -6 to 6
Outputs:
- activations: bfloat16 [256, 262144], P('feat', 'dom')
- grad_input: bfloat16 [256, 262144], P('feat', 'dom')
- grad_weight: float32 [256, 256], P(None, 'feat')
- grad_bias: float32 [256], P('feat')
Inputs may be any that keep to these rules, and one draw needn't show every extreme that they name: `tile_row`: entries past a partition's tile_count are padding, of the same range. `tile_col`: among a partition's valid entries, each peer's halo slot 16 + q is named at most once, and a partition's own slot never. `send_block`: entry q * 128 + p is the local block that partition q sends to partition p; it is defined for every pair.
All inputs are finite; a program needn't handle non-finite values.
Results may differ from a plain program's by a relative error of at most 0.0064.
Values may be sent and summed in bfloat16 or wider, within the bound.
No kernel may reach another device: no remote copies, remote signals or barrier semaphores. Data moves between devices by JAX's collectives and lax.ppermute only.
A program may use at most 64 MiB of HBM per device.

v0:
```python
import math
import jax
import jax.numpy as jnp
from jax import lax
from jax.sharding import PartitionSpec as P


def smooth_gate(values):
    return jax.nn.gelu(values, approximate=True)


def per_device(
    node_feats, weight, bias_vec, adj_tiles, tile_row, tile_col, tile_count, send_block, cotangent
):
    feat_rows, node_rows = node_feats.shape
    tile_slots = adj_tiles.shape[0]
    tile_size = adj_tiles.shape[1]
    blocks = node_rows // tile_size
    domains = lax.axis_size("dom")
    whole = lax.all_gather(node_feats, "feat", axis=0, tiled=True)
    hidden = lax.dot_general(
        weight, whole, (((0,), (0,)), ((), ())), preferred_element_type=jnp.float32
    ).astype(jnp.bfloat16)
    hid_blocks = hidden.reshape(feat_rows, blocks, tile_size)
    outgoing = jnp.take(hid_blocks, send_block, axis=1)
    incoming = lax.all_to_all(outgoing, "dom", split_axis=1, concat_axis=1, tiled=True)
    sources = jnp.concatenate([hid_blocks, incoming], axis=1)
    live_tiles = jnp.arange(tile_slots) < tile_count[0]
    live_float = live_tiles.astype(jnp.float32)
    row_place = (tile_row[:, None] == jnp.arange(blocks)[None, :]).astype(jnp.float32) * live_float[
        :, None
    ]
    picked = jnp.take(sources, tile_col, axis=1)
    products = jnp.einsum("otb,tab->ota", picked, adj_tiles, preferred_element_type=jnp.float32)
    summed = jnp.einsum(
        "ota,tr->ora", products, row_place, precision=lax.Precision.HIGHEST
    ).reshape(feat_rows, node_rows)
    preact = summed + bias_vec.astype(jnp.float32)[:, None]
    activated, pullback = jax.vjp(smooth_gate, preact)
    grad_pre = pullback(cotangent.astype(jnp.float32))[0]
    grad_low = grad_pre.astype(jnp.bfloat16)
    grad_blocks = grad_low.reshape(feat_rows, blocks, tile_size)
    rows_picked = jnp.take(grad_blocks, tile_row, axis=1)
    backward = jnp.einsum(
        "ota,tab->otb", rows_picked, adj_tiles, preferred_element_type=jnp.float32
    )
    src_place = (tile_col[:, None] == jnp.arange(blocks + domains)[None, :]).astype(
        jnp.float32
    ) * live_float[:, None]
    recv_place = (send_block[:, None] == jnp.arange(blocks)[None, :]).astype(jnp.float32)
    own_sum = jnp.einsum(
        "otb,tr->orb", backward, src_place[:, :blocks], precision=lax.Precision.HIGHEST
    )
    slot_hit = jnp.logical_and(
        tile_col[:, None] == blocks + jnp.arange(domains)[None, :], live_tiles[:, None]
    )
    slot_rows = jnp.sum(jnp.where(slot_hit, tile_row[:, None], 0), axis=0)
    out_tiles = jnp.einsum(
        "tq,tab->qab", slot_hit.astype(jnp.bfloat16), adj_tiles, preferred_element_type=jnp.float32
    ).astype(jnp.bfloat16)
    out_rows = jnp.take(grad_blocks, slot_rows, axis=1)
    in_tiles = lax.all_to_all(out_tiles, "dom", split_axis=0, concat_axis=0, tiled=True)
    in_rows = lax.all_to_all(out_rows, "dom", split_axis=1, concat_axis=1, tiled=True)
    remote_sum = jnp.einsum("oqa,qab->oqb", in_rows, in_tiles, preferred_element_type=jnp.float32)
    grad_sum = own_sum + jnp.einsum(
        "oqb,qr->orb", remote_sum, recv_place, precision=lax.Precision.HIGHEST
    )
    grad_hidden = grad_sum.reshape(feat_rows, node_rows).astype(jnp.bfloat16)
    norm_scale = 1.0 / math.sqrt(domains * node_rows)
    weight_part = lax.dot_general(
        whole, grad_hidden, (((1,), (1,)), ((), ())), preferred_element_type=jnp.float32
    )
    bias_part = jnp.sum(grad_pre, axis=1)
    weight_sum, bias_sum = lax.psum((weight_part, bias_part), "dom")
    grad_weight = weight_sum * norm_scale
    grad_bias = bias_sum * norm_scale
    full_weight, all_grad = (
        lax.all_gather(weight, "feat", axis=1, tiled=True),
        lax.all_gather(grad_hidden, "feat", axis=0, tiled=True),
    )
    my_rows = lax.dynamic_slice_in_dim(
        full_weight, lax.axis_index("feat") * feat_rows, feat_rows, 0
    )
    grad_input = jnp.dot(my_rows, all_grad, preferred_element_type=jnp.float32).astype(jnp.bfloat16)
    return (activated.astype(jnp.bfloat16), grad_input, grad_weight, grad_bias)


def solution(mesh):
    placed = (
        P("feat", "dom"),
        P(None, "feat"),
        P("feat"),
        P("dom", None, None),
        P("dom"),
        P("dom"),
        P("dom"),
        P("dom"),
        P("feat", "dom"),
    )
    return jax.shard_map(
        per_device,
        mesh=mesh,
        in_specs=placed,
        out_specs=(P("feat", "dom"), P("feat", "dom"), P(None, "feat"), P("feat")),
        check_vma=False,
    )
```

profile of v0, /device:TPU:1, one launch (start us, length us, event | category | flops | bytes accessed | tf_op | source)
XLA Modules:
  0.0 581.7 jit_solution(17211733674106753430)
XLA Ops:
  7.2 0.0 copy-start
  7.2 0.0 all-gather.3.cloned.1.call-start
  7.2 0.7 all-gather.3.cloned.1.call-update
  7.9 0.9 compare_select_fusion.1
  8.8 0.7 compare_and_fusion.3
  9.4 34.6 %all-gather.3.cloned.1.call-done = bf16[256,2048]{1,0:T(8,128)(2,1)} async-done(((bf16[64,2048]{1,0:T(8,128)(2,1)}), bf16[256,2048]{1,0:T(8,128)(2,1)}) %all-gather.3.cloned.1.call-update) | async-done | bytes 1048592 | tf_op jit(solution)/shard_map/all_gather | solution.py:20
  44.0 1.5 fusion.23
  45.6 0.1 copy.68
  45.6 2.2 gather_fusion.2
  47.8 3.2 select_bitcast_fusion.1
  51.0 0.0 copy-start.5
  51.0 15.8 %all-to-all-start = ((bf16[64,128,128]{2,0,1:T(8,128)(2,1)}), bf16[64,128,128]{2,0,1:T(8,128)(2,1)}, u32[]{:S(2)}, u32[]{:S(2)}) async-start(bf16[64,128,128]{2,0,1:T(8,128)(2,1)} %select_bitcast_fusion.1), calls=%async_computation | async-start | bytes 4194304 | tf_op jit(solution)/shard_map/all_to_all | solution.py:26
  67.5 0.0 copy-done
  67.5 0.0 copy-done.5
  67.5 2.9 fusion.8
  70.4 4.7 copy.30
  75.1 0.0 copy-start.8
  75.1 0.0 copy-start.6
  75.1 42.6 %all-to-all-done = bf16[64,128,128]{2,0,1:T(8,128)(2,1)} async-done(((bf16[64,128,128]{2,0,1:T(8,128)(2,1)}), bf16[64,128,128]{2,0,1:T(8,128)(2,1)}, u32[]{:S(2)}, u32[]{:S(2)}) %all-to-all-start) | async-done | bytes 2097184 | tf_op jit(solution)/shard_map/all_to_all | solution.py:26
  117.7 9.3 %all-to-all-start.1 = ((bf16[128,128,128]{2,1,0:T(8,128)(2,1)}), bf16[128,128,128]{2,1,0:T(8,128)(2,1)}, u32[]{:S(2)}, u32[]{:S(2)}) async-start(bf16[128,128,128]{2,1,0:T(8,128)(2,1)} %copy.30), calls=%async_computation.1 | async-start | bytes 8388608 | tf_op jit(solution)/shard_map/all_to_all | solution.py:62
  127.1 0.0 copy-done.8
  127.1 0.0 copy-done.6
  127.1 0.1 select_reduce_fusion
  127.3 3.3 pad_maximum_fusion
  130.6 3.6 gather_fusion
  134.2 3.6 convolution_bitcast_fusion.2
  137.8 0.0 copy-start.3
  137.8 3.3 fusion.6
  141.1 0.0 copy-done.3
  141.1 1.3 fusion.61
  142.5 0.1 copy_bitcast_fusion.1
  142.6 2.1 gather_fusion.3
  144.7 3.2 select_bitcast_fusion
  147.9 75.7 %all-to-all-done.1 = bf16[128,128,128]{2,1,0:T(8,128)(2,1)} async-done(((bf16[128,128,128]{2,1,0:T(8,128)(2,1)}), bf16[128,128,128]{2,1,0:T(8,128)(2,1)}, u32[]{:S(2)}, u32[]{:S(2)}) %all-to-all-start.1) | async-done | bytes 4194336 | tf_op jit(solution)/shard_map/all_to_all | solution.py:62
  223.6 22.7 %all-to-all-start.2 = ((bf16[64,128,128]{2,0,1:T(8,128)(2,1)}), bf16[64,128,128]{2,0,1:T(8,128)(2,1)}, u32[]{:S(2)}, u32[]{:S(2)}) async-start(bf16[64,128,128]{2,0,1:T(8,128)(2,1)} %select_bitcast_fusion), calls=%async_computation.2 | async-start | bytes 4194304 | tf_op jit(solution)/shard_map/all_to_all | solution.py:63
  246.3 0.3 all-reduce.2.cloned.1.call-start
  246.6 2.0 gather_fusion.1
  248.6 4.1 convolution_bitcast_fusion.1
  252.7 0.0 copy-start.7
  252.7 44.5 %all-to-all-done.2 = bf16[64,128,128]{2,0,1:T(8,128)(2,1)} async-done(((bf16[64,128,128]{2,0,1:T(8,128)(2,1)}), bf16[64,128,128]{2,0,1:T(8,128)(2,1)}, u32[]{:S(2)}, u32[]{:S(2)}) %all-to-all-start.2) | async-done | bytes 2097184 | tf_op jit(solution)/shard_map/all_to_all | solution.py:63
  297.2 4.0 convolution_bitcast_fusion
  301.3 0.0 copy-done.7
  301.3 0.0 copy-start.1
  301.3 3.8 fusion
  305.1 0.0 copy-done.1
  305.1 0.0 copy-start.2
  305.1 0.0 copy-start.4
  305.2 3.3 fusion.20
  308.5 0.0 copy-done.2
  308.5 1.1 convolution_bitcast_fusion.3
  309.5 0.0 all-reduce.2.cloned.1.call-update
  309.6 0.0 all-gather.5.cloned.1.call-start
  309.6 0.8 copy.67
  310.4 0.0 all-gather.5.cloned.1.call-update
  310.4 0.0 copy-done.4
  310.4 9.1 %all_gather.10 = bf16[256,256]{0,1:T(8,128)(2,1)S(1)} all-gather(bf16[256,64]{0,1:T(8,128)(2,1)S(1)} %copy-done.4), channel_id=1, replica_groups=mesh['dom'=128,'feat'=4] {'feat'}, dimensions={1}, use_global_device_ids=true | all-gather | bytes 163840 | tf_op jit(solution)/shard_map/all_gather | solution.py:78
  319.5 251.3 %psum.15 = f32[64]{0:T(128)S(1)} all-reduce(f32[64]{0:T(128)S(1)} %get-tuple-element.5), channel_id=1, replica_groups=mesh['dom'=128,'feat'=4] {'dom'}, use_global_device_ids=true, to_apply=%region_3.5 | all-reduce | flops 64 | bytes 512 | tf_op jit(solution)/shard_map/psum | solution.py:74
  570.8 0.5 broadcast_multiply_fusion.1
  571.3 0.0 all-reduce.2.cloned.1.call-done
  571.3 1.5 broadcast_multiply_fusion
  572.8 0.0 all-gather.5.cloned.1.call-done
  572.8 2.3 convolution_convert_fusion
  (14 shorter events, 0.1 us)
Async XLA Ops:
  7.2 60.3 %copy-start = (bf16[96,128,128]{2,1,0:T(8,128)(2,1)S(1)}, bf16[96,128,128]{2,1,0:T(8,128)(2,1)}, u32[]{:S(2)}) copy-start(bf16[96,128,128]{2,1,0:T(8,128)(2,1)} %param.14) | copy-start | bytes 9437188
  7.2 36.8 %all-gather.3.cloned.1.call-start = ((), (), s32[]{:S(2)}) async-start(), calls=%async_computation.3 | async-start | bytes 1310720 | tf_op jit(solution)/shard_map/all_gather | solution.py:20
  51.0 16.5 %copy-start.5 = (s32[96]{0:T(128)S(1)}, s32[96]{0:T(128)}, u32[]{:S(2)}) copy-start(s32[96]{0:T(128)} %param.16) | copy-start | bytes 1156
  51.0 66.7 %all-to-all-start = ((bf16[64,128,128]{2,0,1:T(8,128)(2,1)}), bf16[64,128,128]{2,0,1:T(8,128)(2,1)}, u32[]{:S(2)}, u32[]{:S(2)}) async-start(bf16[64,128,128]{2,0,1:T(8,128)(2,1)} %select_bitcast_fusion.1), calls=%async_computation | async-start | bytes 4194304 | tf_op jit(solution)/shard_map/all_to_all | solution.py:26
  75.1 52.0 %copy-start.8 = (bf16[64]{0:T(256)(128)(2,1)S(1)}, bf16[64]{0:T(256)(128)(2,1)}, u32[]{:S(2)}) copy-start(bf16[64]{0:T(256)(128)(2,1)} %param.13) | copy-start | bytes 388
  75.1 52.0 %copy-start.6 = (s32[96]{0:T(128)S(1)}, s32[96]{0:T(128)}, u32[]{:S(2)}) copy-start(s32[96]{0:T(128)} %param.15) | copy-start | bytes 1156
  117.7 105.8 %all-to-all-start.1 = ((bf16[128,128,128]{2,1,0:T(8,128)(2,1)}), bf16[128,128,128]{2,1,0:T(8,128)(2,1)}, u32[]{:S(2)}, u32[]{:S(2)}) async-start(bf16[128,128,128]{2,1,0:T(8,128)(2,1)} %copy.30), calls=%async_computation.1 | async-start | bytes 8388608 | tf_op jit(solution)/shard_map/all_to_all | solution.py:62
  137.8 3.3 copy-start.3
  223.6 73.6 %all-to-all-start.2 = ((bf16[64,128,128]{2,0,1:T(8,128)(2,1)}), bf16[64,128,128]{2,0,1:T(8,128)(2,1)}, u32[]{:S(2)}, u32[]{:S(2)}) async-start(bf16[64,128,128]{2,0,1:T(8,128)(2,1)} %select_bitcast_fusion), calls=%async_computation.2 | async-start | bytes 4194304 | tf_op jit(solution)/shard_map/all_to_all | solution.py:63
  246.3 325.0 %all-reduce.2.cloned.1.call-start = ((), (), s32[]{:S(2)}) async-start(), calls=%async_computation.5 | async-start | bytes 131072 | tf_op jit(solution)/shard_map/psum | solution.py:74
  252.7 48.5 %copy-start.7 = (s32[128]{0:T(128)S(1)}, s32[128]{0:T(128)}, u32[]{:S(2)}) copy-start(s32[128]{0:T(128)} %param.18) | copy-start | bytes 1540
  301.3 3.9 copy-start.1
  305.1 3.3 copy-start.2
  305.1 5.3 copy-start.4
  309.6 263.2 %all-gather.5.cloned.1.call-start = ((), (), s32[]{:S(2)}) async-start(), calls=%async_computation.4 | async-start | bytes 1310720 | tf_op jit(solution)/shard_map/all_gather | solution.py:79
Sparse Core Ops, SparseCore 0:
  10.1 33.8 all-gather.2
  309.7 175.5 all-reduce.1
  488.0 21.2 all-gather.4
where the time goes:
time: 582 us
  blocking collectives  260 us (45%)
  waiting for transfers between devices  198 us (34%)
  starting transfers between devices  48.1 us (8%)
  matrix products  30.1 us (5%)
  local copies, waits for them, and re-layouts  15.6 us (3%)
  other arithmetic  14.7 us (3%)
  between operations  14.7 us (3%)
    psum x1, blocking collectives, per_device(): weight_sum, bias_sum = lax.psum((weight_part, bias_part), 'dom')  251 us
    all_to_all x1, waiting for transfers between devices, per_device(): lax.all_to_all(out_tiles, 'dom', split_axis=0, concat_axis=0, tiled=True)  75.7 us
    all_to_all x1, waiting for transfers between devices, per_device(): lax.all_to_all(out_rows, 'dom', split_axis=1, concat_axis=1, tiled=True)  44.5 us
    all_to_all x1, waiting for transfers between devices, per_device(): lax.all_to_all(outgoing, 'dom', split_axis=1, concat_axis=1, tiled=True)  42.6 us
    all_gather x1, waiting for transfers between devices, per_device(): whole = lax.all_gather(node_feats, 'feat', axis=0, tiled=True)  34.6 us
    all_to_all x1, starting transfers between devices, per_device(): lax.all_to_all(out_rows, 'dom', split_axis=1, concat_axis=1, tiled=True)  22.7 us
    all_to_all x1, starting transfers between devices, per_device(): lax.all_to_all(outgoing, 'dom', split_axis=1, concat_axis=1, tiled=True)  15.8 us
  transfers between devices with their start and end apart: 6, of which 4 were waited for; matrix products, arithmetic and copies ran while one was open for 7% of the time, Pallas kernels for 0%

commit v1 on v0

--- a/solution.py
+++ b/solution.py
@@ -17,7 +17,12 @@
     tile_size = adj_tiles.shape[1]
     blocks = node_rows // tile_size
     domains = lax.axis_size("dom")
-    whole = lax.all_gather(node_feats, "feat", axis=0, tiled=True)
+    ring = [node_feats]
+    for hop in range(3):
+        ring.append(lax.ppermute(ring[-1], "feat", [(dev, (dev + 1) % 4) for dev in range(4)]))
+    whole = jnp.roll(
+        jnp.concatenate(ring[::-1], axis=0), (lax.axis_index("feat") + 1) * ring[0].shape[0], axis=0
+    )
     hidden = lax.dot_general(
         weight, whole, (((0,), (0,)), ((), ())), preferred_element_type=jnp.float32
     ).astype(jnp.bfloat16)

time: 582 us -> 589 us (1.012)
  waiting for transfers between devices: 198 us -> 181 us
  starting transfers between devices: 48.1 us -> 63.9 us
  local copies, waits for them, and re-layouts: 15.6 us -> 23.5 us
    all_gather x1 -> x0, waiting for transfers between devices: 34.6 us -> none  [per_device(): whole = lax.all_gather(node_feats, 'feat', axis=0, tiled=True)]
    ppermute x0 -> x3, waiting for transfers between devices: none -> 17.8 us  [per_device(): lax.ppermute(ring[-1], 'feat', [(dev, (dev + 1) % 4) for dev in range(4)])]
    ppermute x0 -> x3, starting transfers between devices: none -> 9.28 us  [per_device(): lax.ppermute(ring[-1], 'feat', [(dev, (dev + 1) % 4) for dev in range(4)])]
    unnamed x19 -> x34, local copies, waits for them, and re-layouts: 0.82 us -> 8.7 us
    all_to_all x1, starting transfers between devices: 15.8 us -> 22.3 us  [per_device(): lax.all_to_all(outgoing, 'dom', split_axis=1, concat_axis=1, tiled=True)]
  transfers between devices with their start and end apart: 6 -> 8, of which waited for: 4 -> 6; matrix products, arithmetic and copies ran while one was open for 7% -> 7% of each run, Pallas kernels for 0% -> 0%
where the time goes in v1:
time: 589 us; the launch traced here: 588 us
  blocking collectives  260 us (44%)
  waiting for transfers between devices  181 us (31%)
  starting transfers between devices  63.9 us (11%)
  matrix products  28.8 us (5%)
  local copies, waits for them, and re-layouts  23.5 us (4%)
  between operations  16.5 us (3%)
  other arithmetic  14.5 us (2%)
    psum x1, blocking collectives, per_device(): weight_sum, bias_sum = lax.psum((weight_part, bias_part), 'dom')  251 us
    all_to_all x1, waiting for transfers between devices, per_device(): lax.all_to_all(out_tiles, 'dom', split_axis=0, concat_axis=0, tiled=True)  75.8 us
    all_to_all x1, waiting for transfers between devices, per_device(): lax.all_to_all(out_rows, 'dom', split_axis=1, concat_axis=1, tiled=True)  44.5 us
    all_to_all x1, waiting for transfers between devices, per_device(): lax.all_to_all(outgoing, 'dom', split_axis=1, concat_axis=1, tiled=True)  42.6 us
    all_to_all x1, starting transfers between devices, per_device(): lax.all_to_all(out_rows, 'dom', split_axis=1, concat_axis=1, tiled=True)  22.7 us
    all_to_all x1, starting transfers between devices, per_device(): lax.all_to_all(outgoing, 'dom', split_axis=1, concat_axis=1, tiled=True)  22.3 us
    ppermute x3, waiting for transfers between devices, per_device(): lax.ppermute(ring[-1], 'feat', [(dev, (dev + 1) % 4) for dev in range(4)])  17.8 us
  transfers between devices with their start and end apart: 8, of which 6 were waited for; matrix products, arithmetic and copies ran while one was open for 7% of the time, Pallas kernels for 0%

profile of v1, /device:TPU:1, one launch (start us, length us, event | category | flops | bytes accessed | tf_op | source)
XLA Modules:
  0.0 588.2 jit_solution(17329568482436748333)
XLA Ops:
  8.0 0.0 copy-start
  8.0 0.0 copy-start.4
  8.0 4.2 collective-permute-start
  12.2 5.2 collective-permute-done
  17.5 0.7 copy-done.5
  18.2 3.2 collective-permute-start.1
  21.3 0.7 compare_select_fusion.1
  22.0 5.3 collective-permute-done.1
  27.3 1.9 collective-permute-start.2
  29.3 0.0 copy-start.6
  29.3 0.7 compare_and_fusion.3
  30.0 7.2 %collective-permute-done.2 = bf16[64,2048]{1,0:T(8,128)(2,1)} collective-permute-done((bf16[64,2048]{1,0:T(8,128)(2,1)}, bf16[64,2048]{1,0:T(8,128)(2,1)}, u32[]{:S(2)}, u32[]{:S(2)}) %collective-permute-start.2) | collective-permute-done | bytes 262176 | tf_op jit(solution)/shard_map/ppermute | solution.py:22
  37.2 1.0 constant_dynamic-update-slice_fusion.7
  38.2 1.0 constant_dynamic-update-slice_fusion.6
  39.2 1.0 constant_dynamic-update-slice_fusion.5
  40.2 1.0 constant_dynamic-update-slice_fusion.4
  41.1 1.0 constant_dynamic-update-slice_fusion.3
  42.1 1.0 constant_dynamic-update-slice_fusion.2
  43.1 0.0 copy-done.6
  43.1 0.0 copy-done.4
  43.2 0.0 copy-start.2
  43.2 1.3 copy-done.2
  44.5 0.3 fusion.23
  44.8 0.1 copy.68
  44.9 2.1 gather_fusion.2
  47.0 3.2 select_bitcast_fusion.1
  50.2 22.3 %all-to-all-start = ((bf16[64,128,128]{2,0,1:T(8,128)(2,1)}), bf16[64,128,128]{2,0,1:T(8,128)(2,1)}, u32[]{:S(2)}, u32[]{:S(2)}) async-start(bf16[64,128,128]{2,0,1:T(8,128)(2,1)} %select_bitcast_fusion.1), calls=%async_computation | async-start | bytes 4194304 | tf_op jit(solution)/shard_map/all_to_all | solution.py:31
  73.2 0.0 copy-done
  73.2 0.0 copy-done.9
  73.2 2.9 fusion.8
  76.1 4.7 copy.30
  80.8 42.6 %all-to-all-done = bf16[64,128,128]{2,0,1:T(8,128)(2,1)} async-done(((bf16[64,128,128]{2,0,1:T(8,128)(2,1)}), bf16[64,128,128]{2,0,1:T(8,128)(2,1)}, u32[]{:S(2)}, u32[]{:S(2)}) %all-to-all-start) | async-done | bytes 2097184 | tf_op jit(solution)/shard_map/all_to_all | solution.py:31
  123.4 9.3 %all-to-all-start.1 = ((bf16[128,128,128]{2,1,0:T(8,128)(2,1)}), bf16[128,128,128]{2,1,0:T(8,128)(2,1)}, u32[]{:S(2)}, u32[]{:S(2)}) async-start(bf16[128,128,128]{2,1,0:T(8,128)(2,1)} %copy.30), calls=%async_computation.1 | async-start | bytes 8388608 | tf_op jit(solution)/shard_map/all_to_all | solution.py:67
  132.8 0.1 select_reduce_fusion
  133.0 3.2 pad_maximum_fusion
  136.2 3.6 gather_fusion
  139.8 3.6 convolution_bitcast_fusion.2
  143.4 0.0 copy-start.7
  143.4 3.3 fusion.6
  146.7 1.3 fusion.65
  148.1 0.1 copy_bitcast_fusion.1
  148.1 2.1 gather_fusion.3
  150.3 3.2 select_bitcast_fusion
  153.5 75.8 %all-to-all-done.1 = bf16[128,128,128]{2,1,0:T(8,128)(2,1)} async-done(((bf16[128,128,128]{2,1,0:T(8,128)(2,1)}), bf16[128,128,128]{2,1,0:T(8,128)(2,1)}, u32[]{:S(2)}, u32[]{:S(2)}) %all-to-all-start.1) | async-done | bytes 4194336 | tf_op jit(solution)/shard_map/all_to_all | solution.py:67
  229.2 22.7 %all-to-all-start.2 = ((bf16[64,128,128]{2,0,1:T(8,128)(2,1)}), bf16[64,128,128]{2,0,1:T(8,128)(2,1)}, u32[]{:S(2)}, u32[]{:S(2)}) async-start(bf16[64,128,128]{2,0,1:T(8,128)(2,1)} %select_bitcast_fusion), calls=%async_computation.2 | async-start | bytes 4194304 | tf_op jit(solution)/shard_map/all_to_all | solution.py:68
  252.0 0.3 all-reduce.2.cloned.1.call-start
  252.3 2.0 gather_fusion.1
  254.3 4.1 convolution_bitcast_fusion.1
  258.4 44.5 %all-to-all-done.2 = bf16[64,128,128]{2,0,1:T(8,128)(2,1)} async-done(((bf16[64,128,128]{2,0,1:T(8,128)(2,1)}), bf16[64,128,128]{2,0,1:T(8,128)(2,1)}, u32[]{:S(2)}, u32[]{:S(2)}) %all-to-all-start.2) | async-done | bytes 2097184 | tf_op jit(solution)/shard_map/all_to_all | solution.py:68
  302.9 4.0 convolution_bitcast_fusion
  306.9 3.8 fusion
  310.8 0.0 copy-done.1
  310.8 0.0 copy-start.3
  310.8 3.3 fusion.20
  314.1 1.1 fusion.24
  315.2 0.0 all-reduce.2.cloned.1.call-update
  315.2 0.0 all-gather.2.cloned.1.call-start
  315.3 0.8 copy.67
  316.0 0.0 all-gather.2.cloned.1.call-update
  316.1 9.1 %all_gather.6 = bf16[256,256]{0,1:T(8,128)(2,1)S(1)} all-gather(bf16[256,64]{0,1:T(8,128)(2,1)S(1)} %copy-done.8), channel_id=1, replica_groups=mesh['dom'=128,'feat'=4] {'feat'}, dimensions={1}, use_global_device_ids=true | all-gather | bytes 163840 | tf_op jit(solution)/shard_map/all_gather | solution.py:83
  325.2 251.3 %psum.15 = f32[64]{0:T(128)S(1)} all-reduce(f32[64]{0:T(128)S(1)} %get-tuple-element.5), channel_id=1, replica_groups=mesh['dom'=128,'feat'=4] {'dom'}, use_global_device_ids=true, to_apply=%region_3.5 | all-reduce | flops 64 | bytes 512 | tf_op jit(solution)/shard_map/psum | solution.py:79
  576.4 0.5 broadcast_multiply_fusion.1
  577.0 1.5 broadcast_multiply_fusion
  578.4 2.3 convolution_convert_fusion.1
  (31 shorter events, 0.1 us)
Async XLA Ops:
  8.0 65.2 %copy-start = (bf16[96,128,128]{2,1,0:T(8,128)(2,1)S(1)}, bf16[96,128,128]{2,1,0:T(8,128)(2,1)}, u32[]{:S(2)}) copy-start(bf16[96,128,128]{2,1,0:T(8,128)(2,1)} %param.14) | copy-start | bytes 9437188
  8.0 35.1 %copy-start.4 = (bf16[64,2048]{1,0:T(8,128)(2,1)S(1)}, bf16[64,2048]{1,0:T(8,128)(2,1)}, u32[]{:S(2)}) copy-start(bf16[64,2048]{1,0:T(8,128)(2,1)} %param.11) | copy-start | bytes 786436
  8.0 9.4 %collective-permute-start = (bf16[64,2048]{1,0:T(8,128)(2,1)}, bf16[64,2048]{1,0:T(8,128)(2,1)S(1)}, u32[]{:S(2)}, u32[]{:S(2)}) collective-permute-start(bf16[64,2048]{1,0:T(8,128)(2,1)} %param.11), channel_id=1, source_target_pairs={{0,1},{1,2},{2,3},{3,0},{4,5},{5,6},{6,7},{7,4},{8,9},{9,10},{10,1... | collective-permute-start | bytes 786440 | tf_op jit(solution)/shard_map/ppermute | solution.py:22
  17.5 0.7 copy-start.5
  18.2 9.2 %collective-permute-start.1 = (bf16[64,2048]{1,0:T(8,128)(2,1)S(1)}, bf16[64,2048]{1,0:T(8,128)(2,1)}, u32[]{:S(2)}, u32[]{:S(2)}) collective-permute-start(bf16[64,2048]{1,0:T(8,128)(2,1)S(1)} %collective-permute-done), channel_id=1, source_target_pairs={{0,1},{1,2},{2,3},{3,0},{4,5},{5,6},{6,7},{7,4},{8,9},{9,10},{10,1... | collective-permute-start | bytes 786440 | tf_op jit(solution)/shard_map/ppermute | solution.py:22
  27.3 9.9 %collective-permute-start.2 = (bf16[64,2048]{1,0:T(8,128)(2,1)}, bf16[64,2048]{1,0:T(8,128)(2,1)}, u32[]{:S(2)}, u32[]{:S(2)}) collective-permute-start(bf16[64,2048]{1,0:T(8,128)(2,1)} %collective-permute-done.1), channel_id=1, source_target_pairs={{0,1},{1,2},{2,3},{3,0},{4,5},{5,6},{6,7},{7,4},{8,9},{9,10},{10,1... | collective-permute-start | bytes 786440 | tf_op jit(solution)/shard_map/ppermute | solution.py:22
  29.3 13.8 %copy-start.6 = (bf16[64,2048]{1,0:T(8,128)(2,1)S(1)}, bf16[64,2048]{1,0:T(8,128)(2,1)}, u32[]{:S(2)}) copy-start(bf16[64,2048]{1,0:T(8,128)(2,1)} %copy-done.5) | copy-start | bytes 786436
  30.0 14.5 %copy-start.8 = (bf16[256,64]{0,1:T(8,128)(2,1)S(1)}, bf16[256,64]{0,1:T(8,128)(2,1)}, u32[]{:S(2)}) copy-start(bf16[256,64]{0,1:T(8,128)(2,1)} %param.12) | copy-start | bytes 98308
  43.2 1.3 copy-start.2
  50.2 23.0 %copy-start.9 = (s32[96]{0:T(128)S(1)}, s32[96]{0:T(128)}, u32[]{:S(2)}) copy-start(s32[96]{0:T(128)} %param.16) | copy-start | bytes 1156
  50.2 73.2 %all-to-all-start = ((bf16[64,128,128]{2,0,1:T(8,128)(2,1)}), bf16[64,128,128]{2,0,1:T(8,128)(2,1)}, u32[]{:S(2)}, u32[]{:S(2)}) async-start(bf16[64,128,128]{2,0,1:T(8,128)(2,1)} %select_bitcast_fusion.1), calls=%async_computation | async-start | bytes 4194304 | tf_op jit(solution)/shard_map/all_to_all | solution.py:31
  80.8 51.9 %copy-start.12 = (bf16[64]{0:T(256)(128)(2,1)S(1)}, bf16[64]{0:T(256)(128)(2,1)}, u32[]{:S(2)}) copy-start(bf16[64]{0:T(256)(128)(2,1)} %param.13) | copy-start | bytes 388
  80.8 52.0 %copy-start.10 = (s32[96]{0:T(128)S(1)}, s32[96]{0:T(128)}, u32[]{:S(2)}) copy-start(s32[96]{0:T(128)} %param.15) | copy-start | bytes 1156
  123.4 105.8 %all-to-all-start.1 = ((bf16[128,128,128]{2,1,0:T(8,128)(2,1)}), bf16[128,128,128]{2,1,0:T(8,128)(2,1)}, u32[]{:S(2)}, u32[]{:S(2)}) async-start(bf16[128,128,128]{2,1,0:T(8,128)(2,1)} %copy.30), calls=%async_computation.1 | async-start | bytes 8388608 | tf_op jit(solution)/shard_map/all_to_all | solution.py:67
  143.4 3.3 copy-start.7
  229.2 73.6 %all-to-all-start.2 = ((bf16[64,128,128]{2,0,1:T(8,128)(2,1)}), bf16[64,128,128]{2,0,1:T(8,128)(2,1)}, u32[]{:S(2)}, u32[]{:S(2)}) async-start(bf16[64,128,128]{2,0,1:T(8,128)(2,1)} %select_bitcast_fusion), calls=%async_computation.2 | async-start | bytes 4194304 | tf_op jit(solution)/shard_map/all_to_all | solution.py:68
  252.0 325.0 %all-reduce.2.cloned.1.call-start = ((), (), s32[]{:S(2)}) async-start(), calls=%async_computation.4 | async-start | bytes 131072 | tf_op jit(solution)/shard_map/psum | solution.py:79
  258.4 48.6 %copy-start.11 = (s32[128]{0:T(128)S(1)}, s32[128]{0:T(128)}, u32[]{:S(2)}) copy-start(s32[128]{0:T(128)} %param.18) | copy-start | bytes 1540
  306.9 3.9 copy-start.1
  310.8 3.3 copy-start.3
  315.2 263.2 %all-gather.2.cloned.1.call-start = ((), (), s32[]{:S(2)}) async-start(), calls=%async_computation.3 | async-start | bytes 1310720 | tf_op jit(solution)/shard_map/all_gather | solution.py:84
Sparse Core Ops, SparseCore 0:
  315.3 174.1 all-reduce.1
Sparse Core Ops, SparseCore 1:
  318.4 20.8 all-gather.1
